TPU v7x, 128 devices: a whole 4x4x4 slice. The times are simulated.
128 devices in a mesh: row: 16 (over z_lo, x, core), col: 8 (over y, z_hi).
Axes of the slice: x: 4, y: 4, z: 4 (z_hi: 2, z_lo: 2; z = z_hi * 2 + z_lo), core: 2. Of those that a mesh axis runs over, the one named last changes fastest.
Arguments:
- shared_rows: float32 [2048, 16384], P('row', 'col'), may hold values from -0.125 to 0.125
- event_counts: int32 [16], replicated, may hold values from 32 to 128, as said below
- ridge: float32 [16384], P('col'), may hold values from 0.5 to 2
- items: float32 [1024, 16384], P('row', 'col'), may hold values from -6 to 6
- cand_ids: int32 [512], replicated, may hold values from 0 to 1023
- theta: float32 [16384], P('col'), may hold values from -0.046875 to 0.046875
Outputs:
- gram_tile: float32 [16384, 16384], P('row', 'col')
- scores: float32 [512], replicated
Inputs may be any that keep to these rules, and one draw needn't show every extreme that they name: event_counts[s] counts the live slots at the start of row shard s's 128 slots; some shard is full.
All inputs are finite; a program needn't handle non-finite values.
Results may differ from a plain program's by a relative error of at most 0.000068.
Values sent between devices are 32-bit elements; how exact they have to be, the bound alone decides.
No kernel may reach another device: no remote copies, remote signals or barrier semaphores. Data moves between devices by JAX's collectives and lax.ppermute only.
A program may use at most 128 MiB of HBM per device.

v0:
```python
import jax
import jax.numpy as jnp
from jax import lax
from jax.sharding import PartitionSpec as P

F = 16384
high = lax.Precision.HIGHEST


def spread(value, axis, source):
    kept = jnp.where(lax.axis_index(axis) == source, value, 0).astype(value.dtype)
    return lax.psum(kept, axis)


def body(shared_rows, event_counts, ridge, items, cand_ids, theta):
    ratio = lax.axis_size("row") // lax.axis_size("col")
    row_pos = lax.axis_index("row")
    col_pos = lax.axis_index("col")
    width_col = shared_rows.shape[1]
    width_row = width_col // ratio
    ev_slots = shared_rows.shape[0]
    slot = lax.iota(jnp.int32, ev_slots)
    masked = jnp.where((slot < event_counts[row_pos])[:, None], shared_rows, jnp.float32(0.0))
    offset = row_pos % ratio * width_row
    root = row_pos // ratio
    contract = (((0,), (0,)), ((), ()))
    col_all = lax.all_gather(masked, "row", axis=0, tiled=True)
    row_all = spread(lax.dynamic_slice_in_dim(col_all, offset, width_row, 1), "col", root)
    tile = lax.dot_general(
        row_all, col_all, contract, precision=high, preferred_element_type=jnp.float32
    )
    rows_global = row_pos * width_row + lax.broadcasted_iota(jnp.int32, (width_row, width_col), 0)
    cols_global = col_pos * width_col + lax.broadcasted_iota(jnp.int32, (width_row, width_col), 1)
    tile = tile + jnp.where(rows_global == cols_global, ridge[None, :], jnp.float32(0.0))
    items_dev = items.shape[0]
    onehot = (
        cand_ids[:, None] == row_pos * items_dev + lax.iota(jnp.int32, items_dev)[None, :]
    ).astype(jnp.float32)
    picked = jnp.dot(onehot, items, precision=high, preferred_element_type=jnp.float32)
    cand_col = lax.psum(picked, "row")
    across = (((1,), (1,)), ((), ()))
    cand_row = spread(lax.dynamic_slice_in_dim(cand_col, offset, width_row, 1), "col", root)
    image_part = lax.dot_general(
        cand_col, tile, across, precision=high, preferred_element_type=jnp.float32
    )
    image_row = lax.psum(image_part, "col")
    quad = jnp.where(col_pos == 0, jnp.sum(cand_row * image_row, axis=1), jnp.float32(0.0))
    linear = jnp.where(
        row_pos == 0,
        jnp.dot(cand_col, theta, precision=high, preferred_element_type=jnp.float32),
        jnp.float32(0.0),
    )
    quad_all, linear_all = lax.psum((quad, linear), ("row", "col"))
    return (tile, linear_all + jnp.sqrt(quad_all / F))


def solution(mesh):
    return jax.shard_map(
        body,
        mesh=mesh,
        in_specs=(P("row", "col"), P(), P("col"), P("row", "col"), P(), P("col")),
        out_specs=(P("row", "col"), P()),
        check_vma=False,
    )
```

profile of v0, /device:TPU:1, one launch (start us, length us, event | category | flops | bytes accessed | tf_op | source)
XLA Modules:
  0.0 940.3 jit_solution(5957106584917055528)
XLA Ops:
  7.2 0.0 copy-start
  7.2 0.0 all-gather.2.cloned.1.call-start
  7.2 1.3 dynamic_slice.9
  8.5 0.6 iota_compare_fusion
  9.2 2.3 broadcast_select_fusion
  11.5 0.0 all-gather.2.cloned.1.call-update
  11.5 0.0 all-reduce.8.cloned.1.call-start
  11.6 0.0 copy-done
  11.6 4.5 fusion
  16.1 0.0 all-reduce.8.cloned.1.call-update
  16.1 0.0 all-reduce.6.cloned.1.call-start
  16.2 90.8 %all-gather.2.cloned.1.call-done = f32[2048,2048]{1,0:T(8,128)} async-done(((f32[128,2048]{1,0:T(8,128)}), f32[2048,2048]{1,0:T(8,128)}) %all-gather.2.cloned.1.call-update) | async-done | bytes 16777232 | tf_op jit(solution)/shard_map/all_gather | solution.py:27
  107.0 8.7 dynamic-slice_select_fusion
  115.7 0.0 copy-start.3
  115.7 0.0 all-reduce.6.cloned.1.call-update
  115.7 0.0 all-reduce.10.cloned.1.call-start
  115.8 122.9 %all-reduce.8.cloned.1.call-done = f32[512,2048]{1,0:T(8,128)} async-done(((f32[512,2048]{1,0:T(8,128)}), f32[512,2048]{1,0:T(8,128)}) %all-reduce.8.cloned.1.call-update) | async-done | bytes 4194320 | tf_op jit(solution)/shard_map/psum | solution.py:40
  238.7 3.2 dynamic-slice_select_fusion.1
  241.9 343.4 %all-reduce.6.cloned.1.call-done = f32[2048,1024]{1,0:T(8,128)} async-done(((f32[2048,1024]{1,0:T(8,128)}), f32[2048,1024]{1,0:T(8,128)}) %all-reduce.6.cloned.1.call-update) | async-done | bytes 8388624 | tf_op jit(solution)/shard_map/psum | solution.py:12
  585.3 0.0 copy-done.3
  585.3 0.0 copy-start.1
  585.3 67.7 %select_add_fusion = f32[1024,2048]{1,0:T(8,128)S(1)} fusion(f32[2048]{0:T(1024)S(1)} %copy-done.3, s32[2048]{0:T(1024)S(1)} %iota_add_fusion, s32[1024]{0:T(1024)S(1)} %iota_add_fusion.1, f32[2048,1024]{1,0:T(8,128)} %all-reduce.6.cloned.1.call-done, f32[2048,2048]{1,0:T(8,128)} %all-gather.2.cloned.1.call-done), kind=kOutput, calls=%fused_computation | convolution fusion | flops 51545899008 | bytes 33574912 | tf_op jit(solution)/shard_map/dot_general | solution.py:29
  653.1 0.0 copy-start.4
  653.1 3.4 copy-done.4
  656.5 0.0 copy-done.1
  656.5 0.0 copy-start.2
  656.5 15.2 %fusion.5 = f32[512,1024]{1,0:T(8,128)} fusion(f32[512,2048]{1,0:T(8,128)S(1)} %copy-done.1, f32[1024,2048]{1,0:T(8,128)S(1)} %select_add_fusion), kind=kOutput, calls=%fused_computation.17 | convolution fusion | flops 12884901888 | bytes 14680064 | tf_op jit(solution)/shard_map/dot_general | solution.py:43
  671.7 0.0 all-reduce.10.cloned.1.call-update
  671.7 0.0 copy-done.2
  671.7 5.8 fusion.4
  677.5 185.2 %all-reduce.10.cloned.1.call-done = (f32[512,1024]{1,0:T(8,128)}, f32[512,1024]{1,0:T(8,128)}) async-done(((f32[512,1024]{1,0:T(8,128)}, f32[512,1024]{1,0:T(8,128)}), (f32[512,1024]{1,0:T(8,128)}, f32[512,1024]{1,0:T(8,128)})) %all-reduce.10.cloned.1.call-update) | async-done | bytes 4194320 | tf_op jit(solution)/shard_map/psum | solution.py:12
  862.7 2.5 multiply_reduce_fusion
  865.2 67.8 %all-reduce = (f32[512]{0:T(512)S(1)}, f32[512]{0:T(512)S(1)}) all-reduce(f32[512]{0:T(512)S(1)} %broadcast_select_fusion.2, f32[512]{0:T(512)S(1)} %broadcast_select_fusion.1), channel_id=1, replica_groups=mesh['row'=16,'col'=8] {'row','col'}, use_global_device_ids=true, to_apply=%region_2.3 | all-reduce | flops 1024 | bytes 8192 | tf_op jit(solution)/shard_map/psum | solution.py:53
  933.0 0.6 sqrt_add_fusion
  (5 shorter events, 0.0 us)
Async XLA Ops:
  7.2 4.4 copy-start
  7.2 99.8 %all-gather.2.cloned.1.call-start = ((), (), s32[]{:S(2)}) async-start(), calls=%async_computation | async-start | bytes 17825792 | tf_op jit(solution)/shard_map/all_gather | solution.py:27
  11.5 227.2 %all-reduce.8.cloned.1.call-start = ((), (), s32[]{:S(2)}) async-start(), calls=%async_computation.2 | async-start | bytes 8388608 | tf_op jit(solution)/shard_map/psum | solution.py:40
  16.1 569.2 %all-reduce.6.cloned.1.call-start = ((), (), s32[]{:S(2)}) async-start(), calls=%async_computation.1 | async-start | bytes 16777216 | tf_op jit(solution)/shard_map/psum | solution.py:12
  115.7 469.7 %copy-start.3 = (f32[2048]{0:T(1024)S(1)}, f32[2048]{0:T(1024)}, u32[]{:S(2)}) copy-start(f32[2048]{0:T(1024)} %param.8) | copy-start | bytes 24580
  115.7 747.0 %all-reduce.10.cloned.1.call-start = ((), (), s32[]{:S(2)}) async-start(), calls=%async_computation.3 | async-start | bytes 8388608 | tf_op jit(solution)/shard_map/psum | solution.py:12
  585.3 71.1 %copy-start.1 = (f32[512,2048]{1,0:T(8,128)S(1)}, f32[512,2048]{1,0:T(8,128)}, u32[]{:S(2)}) copy-start(f32[512,2048]{1,0:T(8,128)} %all-reduce.8.cloned.1.call-done) | copy-start | bytes 12582916
  653.1 3.4 copy-start.4
  656.5 15.3 %copy-start.2 = (f32[2048]{0:T(1024)S(1)}, f32[2048]{0:T(1024)}, u32[]{:S(2)}) copy-start(f32[2048]{0:T(1024)} %param.11) | copy-start | bytes 24580
Sparse Core Ops, SparseCore 0:
  11.7 95.2 all-gather.1
  109.5 129.1 all-reduce.7
  241.8 343.4 all-reduce.5
  671.8 190.8 all-reduce.9
where the time goes:
time: 944 us; the launch traced here: 940 us
  waiting for transfers between devices  742 us (79%)
  matrix products  93.2 us (10%)
  blocking collectives  67.8 us (7%)
  other arithmetic  18 us (2%)
  between operations  14.1 us (1%)
    psum x2, waiting for transfers between devices, spread(): return lax.psum(kept, axis)  529 us
    psum x1, waiting for transfers between devices, body(): cand_col = lax.psum(picked, 'row')  123 us
    all_gather x1, waiting for transfers between devices, body(): col_all = lax.all_gather(masked, 'row', axis=0, tiled=True)  90.8 us
    psum x1, blocking collectives, body(): quad_all, linear_all = lax.psum((quad, linear), ('row', 'col'))  67.8 us
    dot_general x1, matrix products, body(): lax.dot_general(row_all, col_all, contract, precision=high, preferred_ele...  67.7 us
  transfers between devices with their start and end apart: 4, of which 4 were waited for; matrix products, arithmetic and copies ran while one was open for 2% of the time, Pallas kernels for 0%

commit v1 on v0

--- a/solution.py
+++ b/solution.py
@@ -37,7 +37,7 @@
         cand_ids[:, None] == row_pos * items_dev + lax.iota(jnp.int32, items_dev)[None, :]
     ).astype(jnp.float32)
     picked = jnp.dot(onehot, items, precision=high, preferred_element_type=jnp.float32)
-    cand_col = lax.psum(picked, "row")
+    cand_col = jnp.sum(lax.all_gather(picked, "row"), axis=0)
     across = (((1,), (1,)), ((), ()))
     cand_row = spread(lax.dynamic_slice_in_dim(cand_col, offset, width_row, 1), "col", root)
     image_part = lax.dot_general(

time: 944 us -> 1100 us (1.17)
  waiting for transfers between devices: 742 us -> 890 us
  other arithmetic: 18 us -> 40.9 us
    all_gather x0 -> x1, waiting for transfers between devices: none -> 276 us  [body(): cand_col = jnp.sum(lax.all_gather(picked, 'row'), axis=0)]
    psum x1 -> x0, waiting for transfers between devices: 123 us -> none  [body(): cand_col = lax.psum(picked, 'row')]
    reduce_sum x0 -> x1, other arithmetic: none -> 22.9 us  [body(): cand_col = jnp.sum(lax.all_gather(picked, 'row'), axis=0)]
  transfers between devices with their start and end apart: 4 -> 4, of which waited for: 4 -> 4; matrix products, arithmetic and copies ran while one was open for 2% -> 6% of each run, Pallas kernels for 0% -> 0%
where the time goes in v1:
time: 1100 us
  waiting for transfers between devices  890 us (81%)
  matrix products  86.9 us (8%)
  blocking collectives  67.8 us (6%)
  other arithmetic  40.9 us (4%)
  between operations  13.9 us (1%)
    psum x2, waiting for transfers between devices, spread(): return lax.psum(kept, axis)  519 us
    all_gather x1, waiting for transfers between devices, body(): cand_col = jnp.sum(lax.all_gather(picked, 'row'), axis=0)  276 us
    all_gather x1, waiting for transfers between devices, body(): col_all = lax.all_gather(masked, 'row', axis=0, tiled=True)  95.4 us
    psum x1, blocking collectives, body(): quad_all, linear_all = lax.psum((quad, linear), ('row', 'col'))  67.8 us
    dot_general x1, matrix products, body(): lax.dot_general(row_all, col_all, contract, precision=high, preferred_ele...  59.7 us
    reduce_sum x1, other arithmetic, body(): cand_col = jnp.sum(lax.all_gather(picked, 'row'), axis=0)  22.9 us
  transfers between devices with their start and end apart: 4, of which 4 were waited for; matrix products, arithmetic and copies ran while one was open for 6% of the time, Pallas kernels for 0%

profile of v1, /device:TPU:1, one launch (start us, length us, event | category | flops | bytes accessed | tf_op | source)
XLA Modules:
  0.0 1101.5 jit_solution(2486135744850171027)
XLA Ops:
  7.2 0.0 copy-start
  7.2 0.0 all-gather.4.cloned.1.call-start
  7.2 1.3 dynamic_slice.9
  8.5 0.6 iota_compare_fusion
  9.2 2.3 broadcast_select_fusion
  11.5 0.0 all-gather.4.cloned.1.call-update
  11.5 0.0 all-reduce.5.cloned.1.call-start
  11.6 95.4 %all-gather.4.cloned.1.call-done = f32[2048,2048]{1,0:T(8,128)} async-done(((f32[128,2048]{1,0:T(8,128)}), f32[2048,2048]{1,0:T(8,128)}) %all-gather.4.cloned.1.call-update) | async-done | bytes 16777232 | tf_op jit(solution)/shard_map/all_gather | solution.py:27
  107.0 8.7 dynamic-slice_select_fusion
  115.7 0.0 copy-start.2
  115.7 0.0 copy-start.3
  115.7 0.0 all-reduce.5.cloned.1.call-update
  115.7 0.0 all-gather.6.cloned.1.call-start
  115.8 0.0 copy-done
  115.8 0.6 copy-done.2
  116.3 3.8 fusion
  120.2 0.0 all-gather.6.cloned.1.call-update
  120.2 0.0 all-reduce.7.cloned.1.call-start
  120.3 338.0 %all-reduce.5.cloned.1.call-done = f32[2048,1024]{1,0:T(8,128)} async-done(((f32[2048,1024]{1,0:T(8,128)}), f32[2048,1024]{1,0:T(8,128)}) %all-reduce.5.cloned.1.call-update) | async-done | bytes 8388624 | tf_op jit(solution)/shard_map/psum | solution.py:12
  458.2 0.0 copy-done.3
  458.2 59.7 %select_add_fusion = f32[1024,2048]{1,0:T(8,128)} fusion(f32[2048]{0:T(1024)S(1)} %copy-done.3, s32[2048]{0:T(1024)S(1)} %iota_add_fusion, s32[1024]{0:T(1024)S(1)} %iota_add_fusion.1, f32[2048,1024]{1,0:T(8,128)} %all-reduce.5.cloned.1.call-done, f32[2048,2048]{1,0:T(8,128)} %all-gather.4.cloned.1.call-done), kind=kOutput, calls=%fused_computation | convolution fusion | flops 51545899008 | bytes 33574912 | tf_op jit(solution)/shard_map/dot_general | solution.py:29
  518.0 275.6 %all-gather.6.cloned.1.call-done = f32[8192,2048]{1,0:T(8,128)} async-done(((f32[512,2048]{1,0:T(8,128)}), f32[8192,2048]{1,0:T(8,128)}) %all-gather.6.cloned.1.call-update) | async-done | bytes 67108880 | tf_op jit(solution)/shard_map/all_gather | solution.py:40
  793.6 22.9 %reduce_sum.18 = f32[512,2048]{1,0:T(8,128)} reduce(f32[16,512,2048]{2,1,0:T(8,128)} %bitcast.1, f32[]{:T(128)} %constant.42.clone.1), dimensions={0}, to_apply=%region_1.2 | reduce | flops 15728640 | bytes 71303168 | tf_op jit(solution)/shard_map/reduce_sum | solution.py:40
  816.5 3.2 dynamic-slice_select_fusion.1
  819.7 0.0 copy-start.1
  819.7 17.6 %fusion.5 = f32[512,1024]{1,0:T(8,128)} fusion(f32[512,2048]{1,0:T(8,128)} %reduce_sum.18, f32[1024,2048]{1,0:T(8,128)} %select_add_fusion), kind=kOutput, calls=%fused_computation.17 | convolution fusion | flops 12884901888 | bytes 14680064 | tf_op jit(solution)/shard_map/dot_general | solution.py:43
  837.3 0.0 all-reduce.7.cloned.1.call-update
  837.3 0.0 copy-done.1
  837.3 5.8 fusion.4
  843.1 181.0 %all-reduce.7.cloned.1.call-done = (f32[512,1024]{1,0:T(8,128)}, f32[512,1024]{1,0:T(8,128)}) async-done(((f32[512,1024]{1,0:T(8,128)}, f32[512,1024]{1,0:T(8,128)}), (f32[512,1024]{1,0:T(8,128)}, f32[512,1024]{1,0:T(8,128)})) %all-reduce.7.cloned.1.call-update) | async-done | bytes 4194320 | tf_op jit(solution)/shard_map/psum | solution.py:12
  1024.0 2.5 multiply_reduce_fusion
  1026.5 67.8 %all-reduce = (f32[512]{0:T(512)S(1)}, f32[512]{0:T(512)S(1)}) all-reduce(f32[512]{0:T(512)S(1)} %broadcast_select_fusion.2, f32[512]{0:T(512)S(1)} %broadcast_select_fusion.1), channel_id=1, replica_groups=mesh['row'=16,'col'=8] {'row','col'}, use_global_device_ids=true, to_apply=%region_2.3 | all-reduce | flops 1024 | bytes 8192 | tf_op jit(solution)/shard_map/psum | solution.py:53
  1094.3 0.6 sqrt_add_fusion
  (5 shorter events, 0.0 us)
Async XLA Ops:
  7.2 108.6 %copy-start = (f32[64,2048]{1,0:T(8,128)S(1)}, f32[64,2048]{1,0:T(8,128)}, u32[]{:S(2)}) copy-start(f32[64,2048]{1,0:T(8,128)} %param.9) | copy-start | bytes 1572868
  7.2 99.8 %all-gather.4.cloned.1.call-start = ((), (), s32[]{:S(2)}) async-start(), calls=%async_computation | async-start | bytes 17825792 | tf_op jit(solution)/shard_map/all_gather | solution.py:27
  11.5 446.7 %all-reduce.5.cloned.1.call-start = ((), (), s32[]{:S(2)}) async-start(), calls=%async_computation.1 | async-start | bytes 16777216 | tf_op jit(solution)/shard_map/psum | solution.py:12
  115.7 0.7 copy-start.2
  115.7 342.6 %copy-start.3 = (f32[2048]{0:T(1024)S(1)}, f32[2048]{0:T(1024)}, u32[]{:S(2)}) copy-start(f32[2048]{0:T(1024)} %param.8) | copy-start | bytes 24580
  115.7 677.9 %all-gather.6.cloned.1.call-start = ((), (), s32[]{:S(2)}) async-start(), calls=%async_computation.2 | async-start | bytes 71303168 | tf_op jit(solution)/shard_map/all_gather | solution.py:40
  120.2 903.9 %all-reduce.7.cloned.1.call-start = ((), (), s32[]{:S(2)}) async-start(), calls=%async_computation.3 | async-start | bytes 8388608 | tf_op jit(solution)/shard_map/psum | solution.py:12
  819.7 17.6 %copy-start.1 = (f32[2048]{0:T(1024)S(1)}, f32[2048]{0:T(1024)}, u32[]{:S(2)}) copy-start(f32[2048]{0:T(1024)} %param.11) | copy-start | bytes 24580
Sparse Core Ops, SparseCore 0:
  11.7 95.2 all-gather.3
  115.8 342.3 all-reduce.4
  459.9 333.5 all-gather.5
  837.4 186.5 all-reduce.6
